TPU v7x, 128 devices: a whole 4x4x4 slice. The times are simulated.
128 devices in a mesh: expert: 16 (over z, x), dp: 8 (over y, core).
Axes of the slice: x: 4, y: 4, z: 4, core: 2. Of those that a mesh axis runs over, the one named last changes fastest.
Arguments:
- tokens: bfloat16 [16, 480, 7168], P('expert', 'dp'), may hold values from -6 to 6
- cotangent: bfloat16 [16, 480, 7168], P('expert', 'dp'), may hold values from -1.5 to 1.5
- counts: int32 [16, 8], replicated, may hold values from 1 to 60, as said below
- w_gate: bfloat16 [16, 7168, 2048], P('expert', None, 'dp'), may hold values from -0.0625 to 0.0625
- w_up: bfloat16 [16, 7168, 2048], P('expert', None, 'dp'), may hold values from -0.0625 to 0.0625
- w_down: bfloat16 [16, 2048, 7168], P('expert', 'dp'), may hold values from -0.125 to 0.125
Outputs:
- outputs: bfloat16 [16, 480, 7168], P('expert', 'dp')
- input_grads: bfloat16 [16, 480, 7168], P('expert', 'dp')
- gate_grad: bfloat16 [16, 7168, 2048], P('expert', None, 'dp')
- up_grad: bfloat16 [16, 7168, 2048], P('expert', None, 'dp')
- down_grad: bfloat16 [16, 2048, 7168], P('expert', 'dp')
Inputs may be any that keep to these rules, and one draw needn't show every extreme that they name: For each expert e below 8, exactly one of experts e and e + 8 is hot: all its counts exceed 40 - 20 and one equals 60; every count of the other is at most 20 and one equals 20.
All inputs are finite; a program needn't handle non-finite values.
Results may differ from a plain program's by a relative error of at most 0.012.
Values may be sent and summed in bfloat16 or wider, within the bound.
No kernel may reach another device: no remote copies, remote signals or barrier semaphores. Data moves between devices by JAX's collectives and lax.ppermute only.
A program may use at most 192 MiB of HBM per device.

v0:
```python
import jax
import jax.numpy as jnp
from jax import lax
from jax.sharding import PartitionSpec as P


def silu_slope(value):
    sigma = jax.nn.sigmoid(value)
    return sigma * (1.0 + value * (1.0 - sigma))


def contract_last(left, right):
    return lax.dot_general(
        left, right, (((1,), (1,)), ((), ())), preferred_element_type=jnp.float32
    )


def contract_first(left, right):
    return lax.dot_general(
        left, right, (((0,), (0,)), ((), ())), preferred_element_type=jnp.float32
    )


def expert_work(rows, cot_rows, gate_w, up_w, down_w):
    gate = jnp.dot(rows, gate_w, preferred_element_type=jnp.float32)
    up = jnp.dot(rows, up_w, preferred_element_type=jnp.float32)
    active = jax.nn.silu(gate)
    hidden = (active * up).astype(jnp.bfloat16)
    out_part = jnp.dot(hidden, down_w, preferred_element_type=jnp.float32).astype(jnp.bfloat16)
    out_part, hidden, gate, up = lax.optimization_barrier((out_part, hidden, gate, up))
    active = jax.nn.silu(gate)
    hidden_grad = contract_last(cot_rows, down_w)
    gate_act = (hidden_grad * up * silu_slope(gate)).astype(jnp.bfloat16)
    up_act = (hidden_grad * active).astype(jnp.bfloat16)
    in_part = contract_last(gate_act, gate_w) + contract_last(up_act, up_w)
    gate_term = contract_first(rows, gate_act)
    up_term = contract_first(rows, up_act)
    down_term = contract_first(hidden, cot_rows)
    return (out_part, in_part, gate_term, up_term, down_term)


def shards(tokens, cotangent, counts, w_gate, w_up, w_down):
    rows_in = tokens[0]
    cot_in = cotangent[0]
    gate_w = w_gate[0]
    up_w = w_up[0]
    down_w = w_down[0]
    expert_pos = lax.axis_index("expert")
    batch_pos = lax.axis_index("dp")
    expert_ids = jnp.arange(counts.shape[0], dtype=jnp.int32)
    batch_ids = jnp.arange(counts.shape[1], dtype=jnp.int32)
    own_counts = jnp.sum(jnp.where(expert_ids[:, None] == expert_pos, counts, 0), axis=0)
    own_total = jnp.sum(jnp.where(batch_ids == batch_pos, own_counts, 0))
    slots = rows_in.shape[0]
    valid = (jnp.arange(slots, dtype=jnp.int32) < own_total)[:, None]
    masked = jnp.where(valid, rows_in, jnp.zeros_like(rows_in))
    masked_cot = jnp.where(valid, cot_in, jnp.zeros_like(cot_in))
    all_rows = lax.all_gather(masked, "dp", axis=0, tiled=True)
    all_cot = lax.all_gather(masked_cot, "dp", axis=0, tiled=True)
    out_part, in_part, gate_term, up_term, down_term = expert_work(
        all_rows, all_cot, gate_w, up_w, down_w
    )
    groups = lax.axis_size("dp")
    outputs = lax.psum_scatter(
        out_part.reshape(groups, slots, -1), "dp", scatter_dimension=0, tiled=False
    )
    input_grads = lax.psum_scatter(
        in_part.astype(jnp.bfloat16).reshape(groups, slots, -1),
        "dp",
        scatter_dimension=0,
        tiled=False,
    )
    gate_grad = gate_term.astype(jnp.bfloat16)
    up_grad = up_term.astype(jnp.bfloat16)
    down_grad = down_term.astype(jnp.bfloat16)
    return (outputs[None], input_grads[None], gate_grad[None], up_grad[None], down_grad[None])


def solution(mesh):
    placed = (
        P("expert", "dp", None),
        P("expert", "dp", None),
        P(),
        P("expert", None, "dp"),
        P("expert", None, "dp"),
        P("expert", "dp", None),
    )
    return jax.shard_map(
        shards,
        mesh=mesh,
        in_specs=placed,
        out_specs=(
            P("expert", "dp", None),
            P("expert", "dp", None),
            P("expert", None, "dp"),
            P("expert", None, "dp"),
            P("expert", "dp", None),
        ),
        check_vma=False,
    )
```

profile of v0, /device:TPU:1, one launch (start us, length us, event | category | flops | bytes accessed | tf_op | source)
XLA Modules:
  0.0 215.1 jit_solution(16203403560469040614)
XLA Ops:
  7.2 0.0 all-gather.5.cloned.1.call-start
  7.2 0.8 select_reduce_fusion
  8.0 0.6 fusion.15
  8.7 0.6 iota_compare_fusion.1
  9.3 2.9 %fusion.13 = (bf16[1,60,7168]{2,1,0:T(8,128)(2,1)}, bf16[1,60,7168]{2,1,0:T(8,128)(2,1)}) fusion(bf16[1,60,7168]{2,1,0:T(8,128)(2,1)} %param.7, pred[60]{0:T(512)(128)(4,1)S(1)} %iota_compare_fusion.1, bf16[1,60,7168]{2,1,0:T(8,128)(2,1)} %param.6), kind=kLoop, calls=%fused_computation.19 | loop fusion | flops 860160 | bytes 3440700
  12.2 0.0 all-gather.5.cloned.1.call-update
  12.2 0.0 all-gather.7.cloned.1.call-start
  12.3 0.7 all-gather.7.cloned.1.call-update
  13.0 0.0 reduce-scatter.3.cloned.1.call-start
  13.0 48.2 %all-gather.5.cloned.1.call-done = bf16[8,60,7168]{2,1,0:T(8,128)(2,1)} async-done(((bf16[1,60,7168]{2,1,0:T(8,128)(2,1)}), bf16[8,60,7168]{2,1,0:T(8,128)(2,1)}) %all-gather.5.cloned.1.call-update) | async-done | bytes 6881296 | tf_op jit(solution)/shard_map/all_gather | solution.py:58
  61.3 6.9 %reshape.28 = bf16[480,7168]{1,0:T(8,128)(2,1)} reshape(bf16[8,60,7168]{2,1,0:T(8,128)(2,1)} %all-gather.5.cloned.1.call-done) | data formatting | bytes 13762560
  68.2 0.0 copy-start
  68.2 0.0 copy-start.1
  68.2 6.2 %fusion.11 = f32[480,256]{1,0:T(8,128)S(1)} fusion(bf16[480,7168]{1,0:T(8,128)(2,1)} %reshape.28, bf16[1,7168,256]{2,1,0:T(8,128)(2,1)} %param.9), kind=kOutput, calls=%fused_computation.16 | convolution fusion | flops 1761607680 | bytes 11042816 | tf_op jit(solution)/shard_map/dot_general | solution.py:25
  74.3 0.4 copy-done
  74.8 1.6 copy-done.1
  76.4 0.0 copy-start.3
  76.4 1.9 multiply_convert_fusion.2
  78.4 0.1 copy-done.3
  78.4 4.8 %convolution_convert_fusion = bf16[480,7168]{1,0:T(8,128)(2,1)} fusion(bf16[480,256]{1,0:T(8,128)(2,1)S(1)} %get-tuple-element.12, bf16[1,256,7168]{2,1,0:T(8,128)(2,1)S(1)} %copy-done.3), kind=kOutput, calls=%fused_computation.1 | convolution fusion | flops 1765048320 | bytes 10797056 | tf_op jit(solution)/shard_map/dot_general | solution.py:29
  83.2 6.9 %reshape.25 = bf16[8,60,7168]{2,1,0:T(8,128)(2,1)} reshape(bf16[480,7168]{1,0:T(8,128)(2,1)} %convolution_convert_fusion) | data formatting | bytes 13762560 | tf_op jit(solution)/shard_map/reshape | solution.py:65
  90.1 0.0 reduce-scatter.3.cloned.1.call-update
  90.2 0.2 reduce-scatter.5.cloned.1.call-start
  90.4 18.5 %all-gather.7.cloned.1.call-done = bf16[8,60,7168]{2,1,0:T(8,128)(2,1)} async-done(((bf16[1,60,7168]{2,1,0:T(8,128)(2,1)}), bf16[8,60,7168]{2,1,0:T(8,128)(2,1)}) %all-gather.7.cloned.1.call-update) | async-done | bytes 6881296 | tf_op jit(solution)/shard_map/all_gather | solution.py:59
  108.9 6.8 %reshape.30 = bf16[480,7168]{1,0:T(8,128)(2,1)} reshape(bf16[8,60,7168]{2,1,0:T(8,128)(2,1)} %all-gather.7.cloned.1.call-done) | data formatting | bytes 13762560
  115.7 0.0 copy-start.4
  115.7 6.2 %multiply_convert_fusion = (bf16[480,256]{1,0:T(8,128)(2,1)S(1)}, bf16[480,256]{1,0:T(8,128)(2,1)S(1)}) fusion(f32[480,256]{1,0:T(8,128)S(1)} %fusion.11, f32[480,256]{1,0:T(8,128)S(1)} %get-tuple-element.10, bf16[480,7168]{1,0:T(8,128)(2,1)} %reshape.30, bf16[1,256,7168]{2,1,0:T(8,128)(2,1)} %param.11), kind=kOutput, calls=%fused_computation.22 | convolution fusion | flops 1763205120 | bytes 12025856 | tf_op jit(solution)/shard_map/dot_general | solution.py:13
  121.9 0.0 copy-done.4
  121.9 0.0 copy-start.2
  121.9 6.9 %fusion.9 = f32[480,7168]{1,0:T(8,128)} fusion(bf16[480,256]{1,0:T(8,128)(2,1)S(1)} %get-tuple-element.14, bf16[1,7168,256]{2,1,0:T(8,128)(2,1)S(1)} %copy-done.4), kind=kOutput, calls=%fused_computation.14 | convolution fusion | flops 1761607680 | bytes 17678336 | tf_op jit(solution)/shard_map/dot_general | solution.py:13
  128.8 0.0 copy-done.2
  128.8 10.0 %add_convert_fusion = bf16[480,7168]{1,0:T(8,128)(2,1)} fusion(f32[480,7168]{1,0:T(8,128)} %fusion.9, bf16[480,256]{1,0:T(8,128)(2,1)S(1)} %get-tuple-element.13, bf16[1,7168,256]{2,1,0:T(8,128)(2,1)S(1)} %copy-done.2), kind=kOutput, calls=%fused_computation | convolution fusion | flops 1768488960 | bytes 24559616 | tf_op jit(solution)/shard_map/dot_general | solution.py:13
  138.9 7.0 %reshape.26 = bf16[8,60,7168]{2,1,0:T(8,128)(2,1)} reshape(bf16[480,7168]{1,0:T(8,128)(2,1)} %add_convert_fusion) | data formatting | bytes 13762560 | tf_op jit(solution)/shard_map/reshape | solution.py:68
  145.8 0.0 slice-start
  145.8 0.0 reduce-scatter.5.cloned.1.call-update
  145.9 0.0 slice-start.1
  145.9 7.2 %fusion.2 = bf16[1,256,7168]{2,1,0:T(8,128)(2,1)} fusion(bf16[480,256]{1,0:T(8,128)(2,1)S(1)} %get-tuple-element.12, bf16[480,7168]{1,0:T(8,128)(2,1)} %reshape.30), kind=kOutput, calls=%fused_computation.7 | convolution fusion | flops 1763442688 | bytes 10797056 | tf_op jit(solution)/shard_map/dot_general | solution.py:19
  153.1 0.0 slice-done
  153.1 0.0 slice-done.1
  153.1 4.0 %fusion.1 = bf16[1,7168,256]{2,1,0:T(8,128)(2,1)} fusion(bf16[480,7168]{1,0:T(8,128)(2,1)S(1)} %bitcast.50, bf16[480,256]{1,0:T(8,128)(2,1)S(1)} %get-tuple-element.13), kind=kOutput, calls=%fused_computation.6 | convolution fusion | flops 1763442688 | bytes 10797056 | tf_op jit(solution)/shard_map/dot_general | solution.py:19
  157.1 4.0 %fusion = bf16[1,7168,256]{2,1,0:T(8,128)(2,1)} fusion(bf16[480,7168]{1,0:T(8,128)(2,1)S(1)} %bitcast.50, bf16[480,256]{1,0:T(8,128)(2,1)S(1)} %get-tuple-element.14), kind=kOutput, calls=%fused_computation.5 | convolution fusion | flops 1763442688 | bytes 10797056 | tf_op jit(solution)/shard_map/dot_general | solution.py:19
  161.1 0.0 reduce-scatter.3.cloned.1.call-done
  161.1 47.4 %reduce-scatter.5.cloned.1.call-done = bf16[1,60,7168]{2,1,0:T(8,128)(2,1)} async-done(((bf16[8,60,7168]{2,1,0:T(8,128)(2,1)}), bf16[1,60,7168]{2,1,0:T(8,128)(2,1)}) %reduce-scatter.5.cloned.1.call-update) | async-done | bytes 860176 | tf_op jit(solution)/shard_map/reduce_scatter | solution.py:67
  (2 shorter events, 0.0 us)
Async XLA Ops:
  7.2 54.1 %all-gather.5.cloned.1.call-start = ((), (), s32[]{:S(2)}) async-start(), calls=%async_computation.4 | async-start | bytes 8257536 | tf_op jit(solution)/shard_map/all_gather | solution.py:58
  12.2 96.7 %all-gather.7.cloned.1.call-start = ((), (), s32[]{:S(2)}) async-start(), calls=%async_computation.5 | async-start | bytes 8257536 | tf_op jit(solution)/shard_map/all_gather | solution.py:59
  13.0 148.2 %reduce-scatter.3.cloned.1.call-start = ((), (), s32[]{:S(2)}) async-start(), calls=%async_computation.2 | async-start | bytes 8257536 | tf_op jit(solution)/shard_map/reduce_scatter | solution.py:64
  68.2 6.6 %copy-start = (bf16[480,7168]{1,0:T(8,128)(2,1)S(1)}, bf16[480,7168]{1,0:T(8,128)(2,1)}, u32[]{:S(2)}) copy-start(bf16[480,7168]{1,0:T(8,128)(2,1)} %reshape.28) | copy-start | bytes 20643844
  68.2 8.2 %copy-start.1 = (bf16[1,7168,256]{2,1,0:T(8,128)(2,1)S(1)}, bf16[1,7168,256]{2,1,0:T(8,128)(2,1)}, u32[]{:S(2)}) copy-start(bf16[1,7168,256]{2,1,0:T(8,128)(2,1)} %param.10) | copy-start | bytes 11010052
  76.4 2.0 copy-start.3
  90.2 118.4 %reduce-scatter.5.cloned.1.call-start = ((), (), s32[]{:S(2)}) async-start(), calls=%async_computation.3 | async-start | bytes 8257536 | tf_op jit(solution)/shard_map/reduce_scatter | solution.py:67
  115.7 6.2 %copy-start.4 = (bf16[1,7168,256]{2,1,0:T(8,128)(2,1)S(1)}, bf16[1,7168,256]{2,1,0:T(8,128)(2,1)}, u32[]{:S(2)}) copy-start(bf16[1,7168,256]{2,1,0:T(8,128)(2,1)} %param.9) | copy-start | bytes 11010052
  121.9 7.0 %copy-start.2 = (bf16[1,7168,256]{2,1,0:T(8,128)(2,1)S(1)}, bf16[1,7168,256]{2,1,0:T(8,128)(2,1)}, u32[]{:S(2)}) copy-start(bf16[1,7168,256]{2,1,0:T(8,128)(2,1)} %param.10) | copy-start | bytes 11010052
  145.8 7.2 %slice-start = ((s8[6881280]{0:T(1024)(128)(4,1)}), s8[2686976]{0:T(1024)(128)(4,1)S(1)}, s32[]{:S(2)}) async-start(s8[6881280]{0:T(1024)(128)(4,1)} %bitcast.49), calls=%async_computation.6 | async-start | bytes 5373952
  145.9 7.2 %slice-start.1 = ((s8[6881280]{0:T(1024)(128)(4,1)}), s8[4194304]{0:T(1024)(128)(4,1)S(1)}, s32[]{:S(2)}) async-start(s8[6881280]{0:T(1024)(128)(4,1)} %bitcast.49), calls=%async_computation.7 | async-start | bytes 8388608
Sparse Core Ops, SparseCore 0:
  12.3 48.8 all-gather.4
  63.5 45.3 all-gather.6
  111.9 46.6 reduce-scatter.2
  161.4 47.0 reduce-scatter.4
where the time goes:
time: 215 us
  waiting for transfers between devices  115 us (53%)
  matrix products  51.3 us (24%)
  local copies, waits for them, and re-layouts  29.7 us (14%)
  between operations  13.8 us (6%)
  other arithmetic  4.97 us (2%)
    all_gather x1, waiting for transfers between devices, shards(): all_rows = lax.all_gather(masked, 'dp', axis=0, tiled=True)  48.2 us
    reduce_scatter x1, waiting for transfers between devices, shards(): lax.psum_scatter(in_part.astype(jnp.bfloat16).reshape(groups, slots, -1),...  47.4 us
    dot_general x3, matrix products, contract_last(): lax.dot_general(left, right, (((1,), (1,)), ((), ())), preferred_element_...  23.2 us
    all_gather x1, waiting for transfers between devices, shards(): all_cot = lax.all_gather(masked_cot, 'dp', axis=0, tiled=True)  18.5 us
    unnamed x16, local copies, waits for them, and re-layouts  15.9 us
    dot_general x3, matrix products, contract_first(): lax.dot_general(left, right, (((0,), (0,)), ((), ())), preferred_element_...  15.2 us
    reshape x1, local copies, waits for them, and re-layouts, shards(): in_part.astype(jnp.bfloat16).reshape(groups, slots, -1)  6.95 us
    reshape x1, local copies, waits for them, and re-layouts, shards(): out_part.reshape(groups, slots, -1)  6.9 us
  transfers between devices with their start and end apart: 4, of which 3 were waited for; matrix products, arithmetic and copies ran while one was open for 37% of the time, Pallas kernels for 0%

commit v1 on v0

--- a/solution.py
+++ b/solution.py
@@ -56,7 +56,9 @@
     masked = jnp.where(valid, rows_in, jnp.zeros_like(rows_in))
     masked_cot = jnp.where(valid, cot_in, jnp.zeros_like(cot_in))
     all_rows = lax.all_gather(masked, "dp", axis=0, tiled=True)
-    all_cot = lax.all_gather(masked_cot, "dp", axis=0, tiled=True)
+    all_cot = jnp.concatenate(
+        lax.all_to_all(jnp.stack([masked_cot] * lax.axis_size("dp")), "dp", 0, 0), axis=0
+    )
     out_part, in_part, gate_term, up_term, down_term = expert_work(
         all_rows, all_cot, gate_w, up_w, down_w
     )

time: 215 us -> 301 us (1.40)
  blocking collectives: 0 us -> 120 us
  waiting for transfers between devices: 115 us -> 80.6 us
    all_to_all x0 -> x1, blocking collectives: none -> 120 us  [shards(): lax.all_to_all(jnp.stack([masked_cot] * lax.axis_size('dp')), 'dp', 0, 0)]
    all_gather x1 -> x0, waiting for transfers between devices: 18.5 us -> none  [shards(): all_cot = lax.all_gather(masked_cot, 'dp', axis=0, tiled=True)]
    reduce_scatter x1, waiting for transfers between devices: 47.4 us -> 31.6 us  [shards(): lax.psum_scatter(in_part.astype(jnp.bfloat16).reshape(groups, slots, -1),...]
    unnamed x16 -> x17, local copies, waits for them, and re-layouts: 15.9 us -> 9.04 us
    reshape x0 -> x1, local copies, waits for them, and re-layouts: none -> 6.82 us  [shards(): jnp.concatenate(lax.all_to_all(jnp.stack([masked_cot] * lax.axis_size('dp...]
  transfers between devices with their start and end apart: 4 -> 3, of which waited for: 3 -> 2; matrix products, arithmetic and copies ran while one was open for 37% -> 17% of each run, Pallas kernels for 0% -> 0%
where the time goes in v1:
time: 301 us
  blocking collectives  120 us (40%)
  waiting for transfers between devices  80.6 us (27%)
  matrix products  50.8 us (17%)
  local copies, waits for them, and re-layouts  30.4 us (10%)
  between operations  13.8 us (5%)
  other arithmetic  4.46 us (1%)
    all_to_all x1, blocking collectives, shards(): lax.all_to_all(jnp.stack([masked_cot] * lax.axis_size('dp')), 'dp', 0, 0)  120 us
    all_gather x1, waiting for transfers between devices, shards(): all_rows = lax.all_gather(masked, 'dp', axis=0, tiled=True)  49 us
    reduce_scatter x1, waiting for transfers between devices, shards(): lax.psum_scatter(in_part.astype(jnp.bfloat16).reshape(groups, slots, -1),...  31.6 us
    dot_general x3, matrix products, contract_last(): lax.dot_general(left, right, (((1,), (1,)), ((), ())), preferred_element_...  22.8 us
    dot_general x3, matrix products, contract_first(): lax.dot_general(left, right, (((0,), (0,)), ((), ())), preferred_element_...  15.1 us
    unnamed x17, local copies, waits for them, and re-layouts  9.04 us
    reshape x1, local copies, waits for them, and re-layouts, shards(): in_part.astype(jnp.bfloat16).reshape(groups, slots, -1)  6.83 us
    reshape x1, local copies, waits for them, and re-layouts, shards(): jnp.concatenate(lax.all_to_all(jnp.stack([masked_cot] * lax.axis_size('dp...  6.82 us
  transfers between devices with their start and end apart: 3, of which 2 were waited for; matrix products, arithmetic and copies ran while one was open for 17% of the time, Pallas kernels for 0%

profile of v1, /device:TPU:1, one launch (start us, length us, event | category | flops | bytes accessed | tf_op | source)
XLA Modules:
  0.0 300.6 jit_solution(17052125042239862696)
XLA Ops:
  7.2 0.0 all-gather.3.cloned.1.call-start
  7.2 0.8 select_reduce_fusion
  8.0 0.6 fusion.14
  8.7 0.6 iota_compare_fusion.1
  9.3 2.2 fusion.13
  11.6 0.0 all-gather.3.cloned.1.call-update
  11.6 0.0 reduce-scatter.3.cloned.1.call-start
  11.6 49.0 %all-gather.3.cloned.1.call-done = bf16[8,60,7168]{2,1,0:T(8,128)(2,1)} async-done(((bf16[1,60,7168]{2,1,0:T(8,128)(2,1)}), bf16[8,60,7168]{2,1,0:T(8,128)(2,1)}) %all-gather.3.cloned.1.call-update) | async-done | bytes 6881296 | tf_op jit(solution)/shard_map/all_gather | solution.py:58
  60.6 6.9 %reshape.40 = bf16[480,7168]{1,0:T(8,128)(2,1)} reshape(bf16[8,60,7168]{2,1,0:T(8,128)(2,1)} %all-gather.3.cloned.1.call-done) | data formatting | bytes 13762560
  67.5 0.0 copy-start
  67.5 0.0 copy-start.1
  67.5 6.1 %fusion.11 = f32[480,256]{1,0:T(8,128)S(1)} fusion(bf16[480,7168]{1,0:T(8,128)(2,1)} %reshape.40, bf16[1,7168,256]{2,1,0:T(8,128)(2,1)} %param.9), kind=kOutput, calls=%fused_computation.16 | convolution fusion | flops 1761607680 | bytes 11042816 | tf_op jit(solution)/shard_map/dot_general | solution.py:25
  73.6 0.0 copy-done
  73.6 0.9 copy-done.1
  74.5 0.0 copy-start.3
  74.5 1.9 multiply_convert_fusion.2
  76.5 0.1 copy-done.3
  76.6 4.8 %convolution_convert_fusion = bf16[480,7168]{1,0:T(8,128)(2,1)} fusion(bf16[480,256]{1,0:T(8,128)(2,1)S(1)} %get-tuple-element.12, bf16[1,256,7168]{2,1,0:T(8,128)(2,1)S(1)} %copy-done.3), kind=kOutput, calls=%fused_computation.1 | convolution fusion | flops 1765048320 | bytes 10797056 | tf_op jit(solution)/shard_map/dot_general | solution.py:29
  81.4 6.8 %reshape.36 = bf16[8,60,7168]{2,1,0:T(8,128)(2,1)} reshape(bf16[480,7168]{1,0:T(8,128)(2,1)} %convolution_convert_fusion) | data formatting | bytes 13762560 | tf_op jit(solution)/shard_map/reshape | solution.py:67
  88.2 0.0 copy-start.5
  88.2 0.0 reduce-scatter.3.cloned.1.call-update
  88.2 0.0 reduce-scatter.5.cloned.1.call-start
  88.3 1.1 copy-done.5
  89.4 0.1 select_bitcast_fusion
  89.5 0.9 stack.5
  90.4 120.4 %all_to_all.5 = bf16[8,60,7168]{2,1,0:T(8,128)(2,1)} all-to-all(bf16[8,60,7168]{2,1,0:T(8,128)(2,1)S(1)} %stack.5), channel_id=1, replica_groups=mesh['expert'=16,'dp'=8] {'dp'}, dimensions={0} | all-to-all | bytes 13762560 | tf_op jit(solution)/shard_map/all_to_all | solution.py:60
  210.8 6.8 %reshape.37 = bf16[480,7168]{1,0:T(8,128)(2,1)} reshape(bf16[8,60,7168]{2,1,0:T(8,128)(2,1)} %all_to_all.5) | data formatting | bytes 13762560 | tf_op jit(solution)/shard_map/reshape | solution.py:59
  217.6 0.0 copy-start.4
  217.6 6.2 %multiply_convert_fusion = (bf16[480,256]{1,0:T(8,128)(2,1)S(1)}, bf16[480,256]{1,0:T(8,128)(2,1)S(1)}) fusion(f32[480,256]{1,0:T(8,128)S(1)} %fusion.11, f32[480,256]{1,0:T(8,128)S(1)} %get-tuple-element.10, bf16[480,7168]{1,0:T(8,128)(2,1)} %reshape.37, bf16[1,256,7168]{2,1,0:T(8,128)(2,1)} %param.11), kind=kOutput, calls=%fused_computation.21 | convolution fusion | flops 1763205120 | bytes 12025856 | tf_op jit(solution)/shard_map/dot_general | solution.py:13
  223.8 0.0 copy-done.4
  223.8 0.0 copy-start.2
  223.8 6.9 %fusion.9 = f32[480,7168]{1,0:T(8,128)} fusion(bf16[480,256]{1,0:T(8,128)(2,1)S(1)} %get-tuple-element.14, bf16[1,7168,256]{2,1,0:T(8,128)(2,1)S(1)} %copy-done.4), kind=kOutput, calls=%fused_computation.14 | convolution fusion | flops 1761607680 | bytes 17678336 | tf_op jit(solution)/shard_map/dot_general | solution.py:13
  230.7 0.0 copy-done.2
  230.8 9.7 %add_convert_fusion = bf16[480,7168]{1,0:T(8,128)(2,1)} fusion(f32[480,7168]{1,0:T(8,128)} %fusion.9, bf16[480,256]{1,0:T(8,128)(2,1)S(1)} %get-tuple-element.13, bf16[1,7168,256]{2,1,0:T(8,128)(2,1)S(1)} %copy-done.2), kind=kOutput, calls=%fused_computation | convolution fusion | flops 1768488960 | bytes 24559616 | tf_op jit(solution)/shard_map/dot_general | solution.py:13
  240.5 6.8 %reshape.38 = bf16[8,60,7168]{2,1,0:T(8,128)(2,1)} reshape(bf16[480,7168]{1,0:T(8,128)(2,1)} %add_convert_fusion) | data formatting | bytes 13762560 | tf_op jit(solution)/shard_map/reshape | solution.py:70
  247.3 0.0 slice-start
  247.3 0.0 reduce-scatter.5.cloned.1.call-update
  247.3 0.0 slice-start.1
  247.3 7.0 %fusion.2 = bf16[1,256,7168]{2,1,0:T(8,128)(2,1)} fusion(bf16[480,256]{1,0:T(8,128)(2,1)S(1)} %get-tuple-element.12, bf16[480,7168]{1,0:T(8,128)(2,1)} %reshape.37), kind=kOutput, calls=%fused_computation.7 | convolution fusion | flops 1763442688 | bytes 10797056 | tf_op jit(solution)/shard_map/dot_general | solution.py:19
  254.4 0.0 slice-done
  254.4 0.0 slice-done.1
  254.4 4.0 %fusion.1 = bf16[1,7168,256]{2,1,0:T(8,128)(2,1)} fusion(bf16[480,7168]{1,0:T(8,128)(2,1)S(1)} %bitcast.46, bf16[480,256]{1,0:T(8,128)(2,1)S(1)} %get-tuple-element.13), kind=kOutput, calls=%fused_computation.6 | convolution fusion | flops 1763442688 | bytes 10797056 | tf_op jit(solution)/shard_map/dot_general | solution.py:19
  258.4 4.0 %fusion = bf16[1,7168,256]{2,1,0:T(8,128)(2,1)} fusion(bf16[480,7168]{1,0:T(8,128)(2,1)S(1)} %bitcast.46, bf16[480,256]{1,0:T(8,128)(2,1)S(1)} %get-tuple-element.14), kind=kOutput, calls=%fused_computation.5 | convolution fusion | flops 1763442688 | bytes 10797056 | tf_op jit(solution)/shard_map/dot_general | solution.py:19
  262.4 0.0 reduce-scatter.3.cloned.1.call-done
  262.4 31.6 %reduce-scatter.5.cloned.1.call-done = bf16[1,60,7168]{2,1,0:T(8,128)(2,1)} async-done(((bf16[8,60,7168]{2,1,0:T(8,128)(2,1)}), bf16[1,60,7168]{2,1,0:T(8,128)(2,1)}) %reduce-scatter.5.cloned.1.call-update) | async-done | bytes 860176 | tf_op jit(solution)/shard_map/reduce_scatter | solution.py:69
  (2 shorter events, 0.0 us)
Async XLA Ops:
  7.2 53.4 %all-gather.3.cloned.1.call-start = ((), (), s32[]{:S(2)}) async-start(), calls=%async_computation.5 | async-start | bytes 8257536 | tf_op jit(solution)/shard_map/all_gather | solution.py:58
  11.6 250.9 %reduce-scatter.3.cloned.1.call-start = ((), (), s32[]{:S(2)}) async-start(), calls=%async_computation.3 | async-start | bytes 8257536 | tf_op jit(solution)/shard_map/reduce_scatter | solution.py:66
  67.5 6.1 %copy-start = (bf16[480,7168]{1,0:T(8,128)(2,1)S(1)}, bf16[480,7168]{1,0:T(8,128)(2,1)}, u32[]{:S(2)}) copy-start(bf16[480,7168]{1,0:T(8,128)(2,1)} %reshape.40) | copy-start | bytes 20643844
  67.5 7.0 %copy-start.1 = (bf16[1,7168,256]{2,1,0:T(8,128)(2,1)S(1)}, bf16[1,7168,256]{2,1,0:T(8,128)(2,1)}, u32[]{:S(2)}) copy-start(bf16[1,7168,256]{2,1,0:T(8,128)(2,1)} %param.10) | copy-start | bytes 11010052
  74.5 2.0 copy-start.3
  88.2 1.2 copy-start.5
  88.2 205.8 %reduce-scatter.5.cloned.1.call-start = ((), (), s32[]{:S(2)}) async-start(), calls=%async_computation.4 | async-start | bytes 8257536 | tf_op jit(solution)/shard_map/reduce_scatter | solution.py:69
  217.6 6.2 %copy-start.4 = (bf16[1,7168,256]{2,1,0:T(8,128)(2,1)S(1)}, bf16[1,7168,256]{2,1,0:T(8,128)(2,1)}, u32[]{:S(2)}) copy-start(bf16[1,7168,256]{2,1,0:T(8,128)(2,1)} %param.9) | copy-start | bytes 11010052
  223.8 7.0 %copy-start.2 = (bf16[1,7168,256]{2,1,0:T(8,128)(2,1)S(1)}, bf16[1,7168,256]{2,1,0:T(8,128)(2,1)}, u32[]{:S(2)}) copy-start(bf16[1,7168,256]{2,1,0:T(8,128)(2,1)} %param.10) | copy-start | bytes 11010052
  247.3 7.1 %slice-start = ((s8[6881280]{0:T(1024)(128)(4,1)}), s8[2686976]{0:T(1024)(128)(4,1)S(1)}, s32[]{:S(2)}) async-start(s8[6881280]{0:T(1024)(128)(4,1)} %bitcast.45), calls=%async_computation.6 | async-start | bytes 5373952
  247.3 7.1 %slice-start.1 = ((s8[6881280]{0:T(1024)(128)(4,1)}), s8[4194304]{0:T(1024)(128)(4,1)S(1)}, s32[]{:S(2)}) async-start(s8[6881280]{0:T(1024)(128)(4,1)} %bitcast.45), calls=%async_computation.7 | async-start | bytes 8388608
Sparse Core Ops, SparseCore 0:
  11.7 48.8 all-gather.2
  88.3 122.8 reduce-scatter.2
  247.4 46.5 reduce-scatter.4
